TPU v7x, 128 devices: a whole 4x4x4 slice. The times are simulated.
128 devices in a mesh: rows: 8 (over x, core), sub: 16 (over z, y).
Axes of the slice: x: 4, y: 4, z: 4, core: 2. Of those that a mesh axis runs over, the one named last changes fastest.
Arguments:
- vectors: float32 [262144, 1024], P(('rows', 'sub')), may hold values from -40 to 40
- list_ids: int32 [262144], P(('rows', 'sub')), may hold values from 0 to 1023
- coarse: float32 [1024, 1024], replicated, may hold values from -3 to 3
- rotation: float32 [1024, 1024], replicated, may hold values from -0.1875 to 0.1875
- codewords: float32 [16, 256, 64], P('sub'), may hold values from -6 to 6
Outputs:
- codebook: float32 [16, 256, 64], P('sub')
- distortion: float32 [16, 262144], P('sub', 'rows')
All inputs are finite; a program needn't handle non-finite values.
Results may differ from a plain program's by a relative error of at most 0.0003.
Values sent between devices are 32-bit elements; how exact they have to be, the bound alone decides.
No kernel may reach another device: no remote copies, remote signals or barrier semaphores. Data moves between devices by JAX's collectives and lax.ppermute only.
A program may use at most 128 MiB of HBM per device.

v0:
```python
import functools

import jax
import jax.numpy as jnp
from jax import lax
from jax.experimental import pallas as pl
from jax.experimental.pallas import tpu as pltpu
from jax.sharding import PartitionSpec as P

ITERS = 3
BLOCK = 4096
CHUNK_BLOCK = 2048
CHUNKS = 2

smoothing_factor = 16.0
pseudo_count = 1.0

HI = lax.Precision.HIGHEST
LOG2E = 1.4426950408889634


def _scores(c8_ref, bias_ref, xt):
    s = jnp.dot(c8_ref[...], xt, precision=HI, preferred_element_type=jnp.float32)
    return s - bias_ref[...]


def _split(a):
    hi = a.astype(jnp.bfloat16)
    return hi, (a - hi.astype(jnp.float32)).astype(jnp.bfloat16)


def _nt(a, b):
    return lax.dot_general(a, b, (((1,), (1,)), ((), ())), preferred_element_type=jnp.float32)


def _stats_body(c8_ref, bias_ref, xt, acc_ref):
    s = _scores(c8_ref, bias_ref, xt)
    m = jnp.max(s, axis=0, keepdims=True)
    e = jnp.exp2(s - m)
    r = 1.0 / jnp.sum(e, axis=0, keepdims=True)
    y = jnp.concatenate([xt * r, jnp.broadcast_to(r, (8, xt.shape[1]))], axis=0)
    eh, el = _split(e)
    yh, yl = _split(y)
    acc_ref[...] += _nt(eh, yh) + _nt(el, yh) + _nt(eh, yl)


def _dist_body(c8_ref, bias_ref, xt, out_ref):
    s = _scores(c8_ref, bias_ref, xt)
    m = jnp.max(s, axis=0, keepdims=True)
    e = jnp.exp2(s - m)
    l = jnp.sum(e, axis=0, keepdims=True)
    t = jnp.sum(e * s, axis=0, keepdims=True)
    xx = jnp.sum(xt * xt, axis=0, keepdims=True)
    out_ref[...] = (xx - (smoothing_factor / LOG2E) * (t / l)) * (1.0 / xt.shape[0])


def _prep(codebook):
    c8 = codebook * (2.0 * LOG2E / smoothing_factor)
    bias = jnp.sum(codebook * codebook, axis=1, keepdims=True) * (LOG2E / smoothing_factor)
    return c8, bias


def _call(body, xs, codebook, out_spec, out_shape, zero_first, block):
    slabs, ds, slab = xs.shape
    per = block // slab
    k = codebook.shape[0]
    c8, bias = _prep(codebook)

    def kernel(c8_ref, bias_ref, xs_ref, out_ref):
        if zero_first:
            @pl.when(pl.program_id(0) == 0)
            def _():
                out_ref[...] = jnp.zeros_like(out_ref)

        xt = jnp.concatenate([xs_ref[j] for j in range(per)], axis=1)
        body(c8_ref, bias_ref, xt, out_ref)

    return pl.pallas_call(
        kernel,
        grid=(slabs // per,),
        in_specs=[
            pl.BlockSpec((k, ds), lambda i: (0, 0)),
            pl.BlockSpec((k, 1), lambda i: (0, 0)),
            pl.BlockSpec((per, ds, slab), lambda i: (i, 0, 0)),
        ],
        out_specs=out_spec,
        out_shape=out_shape,
        compiler_params=pltpu.CompilerParams(dimension_semantics=("arbitrary",)),
    )(c8, bias, xs)


def soft_stats(xt, codebook, block=BLOCK):
    ds = xt.shape[1]
    k = codebook.shape[0]
    return _call(
        _stats_body,
        xt,
        codebook,
        pl.BlockSpec((k, ds + 8), lambda i: (0, 0)),
        jax.ShapeDtypeStruct((k, ds + 8), jnp.float32),
        True,
        block,
    )


def soft_distortion(xt, codebook):
    n = xt.shape[0] * xt.shape[2]
    return _call(
        _dist_body,
        xt,
        codebook,
        pl.BlockSpec((1, BLOCK), lambda i: (0, i)),
        jax.ShapeDtypeStruct((1, n), jnp.float32),
        False,
        BLOCK,
    )


def gathered_psum(x, axis, size):
    parts = lax.all_to_all(
        jnp.broadcast_to(x[None], (size,) + x.shape), axis, 0, 0, tiled=True
    )
    total = parts[0]
    for j in range(1, size):
        total = total + parts[j]
    return total


def per_device(vectors, list_ids, coarse, rotation, codewords, rows_size, chunks):
    local = vectors.shape[0]
    width = local // chunks
    codebook = codewords[0]
    ds = codebook.shape[1]
    xts = []
    parts = []
    for c in range(chunks):
        rows = slice(c * width, (c + 1) * width)
        residual = vectors[rows] - jnp.take(coarse, list_ids[rows], axis=0)
        if c >= 2:
            residual, parts[c - 2] = lax.optimization_barrier((residual, parts[c - 2]))
        rotated_t = lax.dot_general(
            rotation, residual, (((0,), (1,)), ((), ())), precision=HI
        )
        xt = lax.all_to_all(
            rotated_t.reshape(-1, ds, width), "sub", split_axis=0, concat_axis=0, tiled=True
        )
        xts.append(xt)
        parts.append(soft_stats(xt, codebook, CHUNK_BLOCK))
    acc = parts[0]
    for part in parts[1:]:
        acc = acc + part
    subs = xts[0].shape[0]
    xt = jnp.concatenate(xts, axis=0)
    def refit(codebook, acc):
        acc = gathered_psum(acc, "rows", rows_size)
        membership_scaled = acc[:, :ds]
        masses = acc[:, ds]
        return (membership_scaled + pseudo_count * codebook) / (masses[:, None] + pseudo_count)

    codebook = refit(codebook, acc)
    codebook = lax.fori_loop(
        1, ITERS, lambda _, codebook: refit(codebook, soft_stats(xt, codebook)), codebook
    )
    distortion = soft_distortion(xt, codebook)
    distortion = distortion.reshape(chunks, subs, width).transpose(1, 0, 2).reshape(1, -1)
    return (codebook[None], distortion)


def solution(mesh):
    in_specs = (P(("rows", "sub"), None), P(("rows", "sub")), P(), P(), P("sub", None, None))
    out_specs = (P("sub", None, None), P("sub", "rows"))
    step = jax.shard_map(
        functools.partial(per_device, rows_size=mesh.shape["rows"], chunks=CHUNKS),
        mesh=mesh,
        in_specs=in_specs,
        out_specs=out_specs,
        check_vma=False,
    )
    return step
```

profile of v0, /device:TPU:1, one launch (start us, length us, event | category | flops | bytes accessed | tf_op | source)
XLA Modules:
  0.0 371.9 jit_solution(9751621993502510405)
XLA Ops:
  2.1 8.6 %gather_fusion.1 = f32[1024,1024]{1,0:T(8,128)} fusion(f32[1024,1024]{1,0:T(8,128)} %param.11, s32[1024]{0:T(1024)S(1)} %get-tuple-element.64), kind=kCustom, calls=%fused_computation.1.clone | custom fusion | bytes 8392704 | tf_op jit(solution)/shard_map/jit(_take)/gather | solution.py:138
  10.6 19.4 %fusion.2 = f32[1024,1024]{0,1:T(8,128)} fusion(f32[1024,1024]{1,0:T(8,128)} %param.12, f32[1024,1024]{1,0:T(8,128)} %gather_fusion.1, f32[2048,1024]{1,0:T(8,128)} %param.9, pred[1024]{0:T(1024)(128)(4,1)S(1)} %get-tuple-element.62), kind=kOutput, calls=%fused_computation.17 | convolution fusion | flops 12886999040 | bytes 16778240 | tf_op jit(solution)/shard_map/dot_general | solution.py:141
  30.0 8.6 %all-to-all-start.2 = ((f32[16,64,1024]{2,1,0:T(8,128)}), f32[16,64,1024]{2,1,0:T(8,128)}, u32[]{:S(2)}, u32[]{:S(2)}) async-start(f32[16,64,1024]{2,1,0:T(8,128)} %bitcast.32), calls=%async_computation.2 | async-start | bytes 8388608 | tf_op jit(solution)/shard_map/all_to_all | solution.py:144
  38.7 8.6 %gather_fusion = f32[1024,1024]{1,0:T(8,128)} fusion(f32[1024,1024]{1,0:T(8,128)} %param.11, s32[1024]{0:T(1024)S(1)} %get-tuple-element.65), kind=kCustom, calls=%fused_computation.clone | custom fusion | bytes 8392704 | tf_op jit(solution)/shard_map/jit(_take)/gather | solution.py:138
  47.3 19.3 %fusion.3 = f32[1024,1024]{0,1:T(8,128)} fusion(f32[1024,1024]{1,0:T(8,128)} %param.12, f32[1024,1024]{1,0:T(8,128)} %gather_fusion, f32[2048,1024]{1,0:T(8,128)} %param.9, pred[1024]{0:T(1024)(128)(4,1)S(1)} %get-tuple-element.63), kind=kOutput, calls=%fused_computation.19 | convolution fusion | flops 12886999040 | bytes 16778240 | tf_op jit(solution)/shard_map/dot_general | solution.py:141
  66.6 34.5 %all-to-all-done.2.xs_ref = f32[16,64,1024]{2,1,0:T(8,128)} async-done(((f32[16,64,1024]{2,1,0:T(8,128)}), f32[16,64,1024]{2,1,0:T(8,128)}, u32[]{:S(2)}, u32[]{:S(2)}) %all-to-all-start.2) | async-done | bytes 4194336 | tf_op jit(solution)/shard_map/all_to_all | solution.py:144
  101.1 4.7 %all-to-all-start.1 = ((f32[16,64,1024]{2,1,0:T(8,128)}), f32[16,64,1024]{2,1,0:T(8,128)}, u32[]{:S(2)}, u32[]{:S(2)}) async-start(f32[16,64,1024]{2,1,0:T(8,128)} %bitcast.31), calls=%async_computation.1 | async-start | bytes 8388608 | tf_op jit(solution)/shard_map/all_to_all | solution.py:144
  107.4 24.4 %shard_map.69 = f32[256,72]{1,0:T(8,128)} custom-call(f32[256,64]{1,0:T(8,128)} %get-tuple-element.61.c8_ref, f32[256,1]{1,0:T(8,128)} %copy.22.bias_ref, f32[16,64,1024]{2,1,0:T(8,128)} %all-to-all-done.2.xs_ref), custom_call_target="tpu_custom_call" | custom-call | tf_op jit(solution)/shard_map/pallas_call | solution.py:78
  131.8 33.6 %all-to-all-done.1.xs_ref = f32[16,64,1024]{2,1,0:T(8,128)} async-done(((f32[16,64,1024]{2,1,0:T(8,128)}), f32[16,64,1024]{2,1,0:T(8,128)}, u32[]{:S(2)}, u32[]{:S(2)}) %all-to-all-start.1) | async-done | bytes 4194336 | tf_op jit(solution)/shard_map/all_to_all | solution.py:144
  165.4 24.4 %shard_map.68 = f32[256,72]{1,0:T(8,128)} custom-call(f32[256,64]{1,0:T(8,128)} %get-tuple-element.61.c8_ref, f32[256,1]{1,0:T(8,128)} %copy.22.bias_ref, f32[16,64,1024]{2,1,0:T(8,128)} %all-to-all-done.1.xs_ref), custom_call_target="tpu_custom_call" | custom-call | tf_op jit(solution)/shard_map/pallas_call | solution.py:78
  189.9 0.9 add.78
  190.9 0.8 broadcast_in_dim.15
  191.7 7.1 %all-to-all-start.3 = ((f32[8,256,72]{1,2,0:T(8,128)}), f32[8,256,72]{1,2,0:T(8,128)S(1)}, u32[]{:S(2)}, u32[]{:S(2)}) async-start(f32[8,256,72]{1,2,0:T(8,128)} %broadcast_in_dim.15), calls=%async_computation.3 | async-start | bytes 1179648 | tf_op jit(solution)/shard_map/all_to_all | solution.py:120
  198.8 4.7 %constant_dynamic-update-slice_fusion.1 = f32[32,64,1024]{2,1,0:T(8,128)} fusion(f32[16,64,1024]{2,1,0:T(8,128)} %all-to-all-done.1.xs_ref), kind=kLoop, calls=%fused_computation.40 | loop fusion | bytes 8388608
  203.5 4.7 %constant_dynamic-update-slice_fusion.xs_ref = f32[32,64,1024]{2,1,0:T(8,128)} fusion(f32[32,64,1024]{2,1,0:T(8,128)} %constant_dynamic-update-slice_fusion.1, f32[16,64,1024]{2,1,0:T(8,128)} %all-to-all-done.2.xs_ref), kind=kLoop, calls=%fused_computation.39 | loop fusion | bytes 8388608 | tf_op jit(solution)/shard_map/concatenate | solution.py:153
  210.2 122.8 %while.10 = (s32[]{:T(128)}, f32[256,64]{1,0:T(8,128)S(1)}, f32[32,64,1024]{2,1,0:T(8,128)}, f32[256]{0:T(256)S(1)}, s32[]{:T(128)}) while((s32[]{:T(128)}, f32[256,64]{1,0:T(8,128)S(1)}, f32[32,64,1024]{2,1,0:T(8,128)}, f32[256]{0:T(256)S(1)}, s32[]{:T(128)}) %tuple.41), condition=%wide.region_3.5_spmd, body=%wide.region_1.0_spmd.sunk | while | flops 211202 | bytes 3907677 | solution.py:161
  210.9 0.8 copy.49.bias_ref
  211.7 43.3 %eval_jaxpr.1 = f32[256,72]{1,0:T(8,128)} custom-call(f32[256,64]{1,0:T(8,128)} %broadcast_multiply_fusion.7.c8_ref, f32[256,1]{1,0:T(8,128)} %copy.49.bias_ref, f32[32,64,1024]{2,1,0:T(8,128)} %get-tuple-element.103.xs_ref), custom_call_target="tpu_custom_call" | custom-call | tf_op jit(solution)/shard_map/while/body/eval_jaxpr/pallas_call | solution.py:78
  254.9 1.0 copy.50
  255.9 0.9 broadcast_in_dim.54
  256.8 4.4 %all-to-all-start = ((f32[8,256,72]{1,2,0:T(8,128)}), f32[8,256,72]{1,2,0:T(8,128)S(1)}, u32[]{:S(2)}, u32[]{:S(2)}) async-start(f32[8,256,72]{1,2,0:T(8,128)} %broadcast_in_dim.54), calls=%async_computation | async-start | bytes 1179648 | tf_op jit(solution)/shard_map/while/body/eval_jaxpr/all_to_all | solution.py:120
  261.3 10.0 %all-to-all-done = f32[8,256,72]{1,2,0:T(8,128)S(1)} async-done(((f32[8,256,72]{1,2,0:T(8,128)}), f32[8,256,72]{1,2,0:T(8,128)S(1)}, u32[]{:S(2)}, u32[]{:S(2)}) %all-to-all-start) | async-done | bytes 589856 | tf_op jit(solution)/shard_map/while/body/eval_jaxpr/all_to_all | solution.py:120
  272.3 0.8 copy.49.bias_ref
  273.1 43.3 %eval_jaxpr.1 = f32[256,72]{1,0:T(8,128)} custom-call(f32[256,64]{1,0:T(8,128)} %broadcast_multiply_fusion.7.c8_ref, f32[256,1]{1,0:T(8,128)} %copy.49.bias_ref, f32[32,64,1024]{2,1,0:T(8,128)} %get-tuple-element.103.xs_ref), custom_call_target="tpu_custom_call" | custom-call | tf_op jit(solution)/shard_map/while/body/eval_jaxpr/pallas_call | solution.py:78
  316.4 1.0 copy.50
  317.3 0.9 broadcast_in_dim.54
  318.2 4.4 %all-to-all-start = ((f32[8,256,72]{1,2,0:T(8,128)}), f32[8,256,72]{1,2,0:T(8,128)S(1)}, u32[]{:S(2)}, u32[]{:S(2)}) async-start(f32[8,256,72]{1,2,0:T(8,128)} %broadcast_in_dim.54), calls=%async_computation | async-start | bytes 1179648 | tf_op jit(solution)/shard_map/while/body/eval_jaxpr/all_to_all | solution.py:120
  322.7 10.0 %all-to-all-done = f32[8,256,72]{1,2,0:T(8,128)S(1)} async-done(((f32[8,256,72]{1,2,0:T(8,128)}), f32[8,256,72]{1,2,0:T(8,128)S(1)}, u32[]{:S(2)}, u32[]{:S(2)}) %all-to-all-start) | async-done | bytes 589856 | tf_op jit(solution)/shard_map/while/body/eval_jaxpr/all_to_all | solution.py:120
  334.4 0.8 copy.34.bias_ref
  335.2 33.3 %shard_map.70 = f32[1,32768]{1,0:T(1,128)} custom-call(f32[256,64]{1,0:T(8,128)} %get-tuple-element.59.c8_ref, f32[256,1]{1,0:T(8,128)} %copy.34.bias_ref, f32[32,64,1024]{2,1,0:T(8,128)} %constant_dynamic-update-slice_fusion.xs_ref), custom_call_target="tpu_custom_call" | custom-call | tf_op jit(solution)/shard_map/pallas_call | solution.py:78
  369.0 1.9 reduce.5
  371.0 0.9 reshape.64
  (46 shorter events, 8.9 us)
Async XLA Ops:
  30.0 71.1 %all-to-all-start.2 = ((f32[16,64,1024]{2,1,0:T(8,128)}), f32[16,64,1024]{2,1,0:T(8,128)}, u32[]{:S(2)}, u32[]{:S(2)}) async-start(f32[16,64,1024]{2,1,0:T(8,128)} %bitcast.32), calls=%async_computation.2 | async-start | bytes 8388608 | tf_op jit(solution)/shard_map/all_to_all | solution.py:144
  101.1 4.7 %copy-start.1 = (f32[1,256,64]{1,2,0:T(8,128)S(1)}, f32[1,256,64]{1,2,0:T(8,128)}, u32[]{:S(2)}) copy-start(f32[1,256,64]{1,2,0:T(8,128)} %param.13) | copy-start | bytes 196612
  101.1 64.3 %all-to-all-start.1 = ((f32[16,64,1024]{2,1,0:T(8,128)}), f32[16,64,1024]{2,1,0:T(8,128)}, u32[]{:S(2)}, u32[]{:S(2)}) async-start(f32[16,64,1024]{2,1,0:T(8,128)} %bitcast.31), calls=%async_computation.1 | async-start | bytes 8388608 | tf_op jit(solution)/shard_map/all_to_all | solution.py:144
  131.8 58.0 %copy-start = (f32[256,72]{1,0:T(8,128)S(1)}, f32[256,72]{1,0:T(8,128)}, u32[]{:S(2)}) copy-start(f32[256,72]{1,0:T(8,128)} %shard_map.69) | copy-start | bytes 221188
  191.7 17.2 %all-to-all-start.3 = ((f32[8,256,72]{1,2,0:T(8,128)}), f32[8,256,72]{1,2,0:T(8,128)S(1)}, u32[]{:S(2)}, u32[]{:S(2)}) async-start(f32[8,256,72]{1,2,0:T(8,128)} %broadcast_in_dim.15), calls=%async_computation.3 | async-start | bytes 1179648 | tf_op jit(solution)/shard_map/all_to_all | solution.py:120
  256.8 14.5 %all-to-all-start = ((f32[8,256,72]{1,2,0:T(8,128)}), f32[8,256,72]{1,2,0:T(8,128)S(1)}, u32[]{:S(2)}, u32[]{:S(2)}) async-start(f32[8,256,72]{1,2,0:T(8,128)} %broadcast_in_dim.54), calls=%async_computation | async-start | bytes 1179648 | tf_op jit(solution)/shard_map/while/body/eval_jaxpr/all_to_all | solution.py:120
  318.2 14.5 %all-to-all-start = ((f32[8,256,72]{1,2,0:T(8,128)}), f32[8,256,72]{1,2,0:T(8,128)S(1)}, u32[]{:S(2)}, u32[]{:S(2)}) async-start(f32[8,256,72]{1,2,0:T(8,128)} %broadcast_in_dim.54), calls=%async_computation | async-start | bytes 1179648 | tf_op jit(solution)/shard_map/while/body/eval_jaxpr/all_to_all | solution.py:120
where the time goes:
time: 373 us; the launch traced here: 372 us
  Pallas kernels  169 us (45%)
  waiting for transfers between devices  88.7 us (24%)
  matrix products  38.7 us (10%)
  local copies, waits for them, and re-layouts  38 us (10%)
  starting transfers between devices  29.3 us (8%)
  other arithmetic  7.67 us (2%)
    pallas_call x5, Pallas kernels, _call(): pl.pallas_call(kernel, grid=(slabs // per,), in_specs=[pl.BlockSpec((k, d...  169 us
    all_to_all x2, waiting for transfers between devices, per_device(): lax.all_to_all(rotated_t.reshape(-1, ds, width), 'sub', split_axis=0, con...  68.1 us
    dot_general x2, matrix products, per_device(): lax.dot_general(rotation, residual, (((0,), (1,)), ((), ())), precision=HI)  38.7 us
    all_to_all x3, waiting for transfers between devices, gathered_psum(): lax.all_to_all(jnp.broadcast_to(x[None], (size,) + x.shape), axis, 0, 0,...  20.6 us
    gather x2, local copies, waits for them, and re-layouts, per_device(): residual = vectors[rows] - jnp.take(coarse, list_ids[rows], axis=0)  17.2 us
    all_to_all x3, starting transfers between devices, gathered_psum(): lax.all_to_all(jnp.broadcast_to(x[None], (size,) + x.shape), axis, 0, 0,...  15.9 us
    all_to_all x2, starting transfers between devices, per_device(): lax.all_to_all(rotated_t.reshape(-1, ds, width), 'sub', split_axis=0, con...  13.3 us
  transfers between devices with their start and end apart: 5, of which 5 were waited for; matrix products, arithmetic and copies ran while one was open for 11% of the time, Pallas kernels for 7%

commit v1 on v0

--- a/solution.py
+++ b/solution.py
@@ -9,7 +9,7 @@
 
 ITERS = 3
 BLOCK = 4096
-CHUNK_BLOCK = 2048
+CHUNK_BLOCK = 1024
 CHUNKS = 2
 
 smoothing_factor = 16.0
@@ -145,7 +145,7 @@
             rotated_t.reshape(-1, ds, width), "sub", split_axis=0, concat_axis=0, tiled=True
         )
         xts.append(xt)
-        parts.append(soft_stats(xt, codebook, CHUNK_BLOCK))
+        parts.append(soft_stats(xt, codebook, BLOCK if c == chunks - 1 else CHUNK_BLOCK))
     acc = parts[0]
     for part in parts[1:]:
         acc = acc + part

time: 373 us -> 376 us (level)
  transfers between devices with their start and end apart: 5 -> 5, of which waited for: 5 -> 5; matrix products, arithmetic and copies ran while one was open for 11% -> 10% of each run, Pallas kernels for 7% -> 6%
where the time goes in v1:
time: 376 us; the launch traced here: 375 us
  Pallas kernels  170 us (45%)
  waiting for transfers between devices  90.3 us (24%)
  matrix products  38.7 us (10%)
  local copies, waits for them, and re-layouts  38 us (10%)
  starting transfers between devices  29.5 us (8%)
  other arithmetic  7.67 us (2%)
    pallas_call x5, Pallas kernels, _call(): pl.pallas_call(kernel, grid=(slabs // per,), in_specs=[pl.BlockSpec((k, d...  170 us
    all_to_all x2, waiting for transfers between devices, per_device(): lax.all_to_all(rotated_t.reshape(-1, ds, width), 'sub', split_axis=0, con...  69.7 us
    dot_general x2, matrix products, per_device(): lax.dot_general(rotation, residual, (((0,), (1,)), ((), ())), precision=HI)  38.7 us
    all_to_all x3, waiting for transfers between devices, gathered_psum(): lax.all_to_all(jnp.broadcast_to(x[None], (size,) + x.shape), axis, 0, 0,...  20.6 us
    gather x2, local copies, waits for them, and re-layouts, per_device(): residual = vectors[rows] - jnp.take(coarse, list_ids[rows], axis=0)  17.2 us
    all_to_all x3, starting transfers between devices, gathered_psum(): lax.all_to_all(jnp.broadcast_to(x[None], (size,) + x.shape), axis, 0, 0,...  15.9 us
    all_to_all x2, starting transfers between devices, per_device(): lax.all_to_all(rotated_t.reshape(-1, ds, width), 'sub', split_axis=0, con...  13.5 us
  transfers between devices with their start and end apart: 5, of which 5 were waited for; matrix products, arithmetic and copies ran while one was open for 10% of the time, Pallas kernels for 6%

profile of v1, /device:TPU:1, one launch (start us, length us, event | category | flops | bytes accessed | tf_op | source)
XLA Modules:
  0.0 375.2 jit_solution(10193229844283410504)
XLA Ops:
  2.1 8.6 %gather_fusion.1 = f32[1024,1024]{1,0:T(8,128)} fusion(f32[1024,1024]{1,0:T(8,128)} %param.11, s32[1024]{0:T(1024)S(1)} %get-tuple-element.64), kind=kCustom, calls=%fused_computation.1.clone | custom fusion | bytes 8392704 | tf_op jit(solution)/shard_map/jit(_take)/gather | solution.py:138
  10.6 19.4 %fusion.2 = f32[1024,1024]{0,1:T(8,128)} fusion(f32[1024,1024]{1,0:T(8,128)} %param.12, f32[1024,1024]{1,0:T(8,128)} %gather_fusion.1, f32[2048,1024]{1,0:T(8,128)} %param.9, pred[1024]{0:T(1024)(128)(4,1)S(1)} %get-tuple-element.62), kind=kOutput, calls=%fused_computation.17 | convolution fusion | flops 12886999040 | bytes 16778240 | tf_op jit(solution)/shard_map/dot_general | solution.py:141
  30.0 8.6 %all-to-all-start.2 = ((f32[16,64,1024]{2,1,0:T(8,128)}), f32[16,64,1024]{2,1,0:T(8,128)}, u32[]{:S(2)}, u32[]{:S(2)}) async-start(f32[16,64,1024]{2,1,0:T(8,128)} %bitcast.32), calls=%async_computation.2 | async-start | bytes 8388608 | tf_op jit(solution)/shard_map/all_to_all | solution.py:144
  38.7 8.6 %gather_fusion = f32[1024,1024]{1,0:T(8,128)} fusion(f32[1024,1024]{1,0:T(8,128)} %param.11, s32[1024]{0:T(1024)S(1)} %get-tuple-element.65), kind=kCustom, calls=%fused_computation.clone | custom fusion | bytes 8392704 | tf_op jit(solution)/shard_map/jit(_take)/gather | solution.py:138
  47.3 19.3 %fusion.3 = f32[1024,1024]{0,1:T(8,128)} fusion(f32[1024,1024]{1,0:T(8,128)} %param.12, f32[1024,1024]{1,0:T(8,128)} %gather_fusion, f32[2048,1024]{1,0:T(8,128)} %param.9, pred[1024]{0:T(1024)(128)(4,1)S(1)} %get-tuple-element.63), kind=kOutput, calls=%fused_computation.19 | convolution fusion | flops 12886999040 | bytes 16778240 | tf_op jit(solution)/shard_map/dot_general | solution.py:141
  66.6 34.5 %all-to-all-done.2.xs_ref = f32[16,64,1024]{2,1,0:T(8,128)} async-done(((f32[16,64,1024]{2,1,0:T(8,128)}), f32[16,64,1024]{2,1,0:T(8,128)}, u32[]{:S(2)}, u32[]{:S(2)}) %all-to-all-start.2) | async-done | bytes 4194336 | tf_op jit(solution)/shard_map/all_to_all | solution.py:144
  101.1 4.9 %all-to-all-start.1 = ((f32[16,64,1024]{2,1,0:T(8,128)}), f32[16,64,1024]{2,1,0:T(8,128)}, u32[]{:S(2)}, u32[]{:S(2)}) async-start(f32[16,64,1024]{2,1,0:T(8,128)} %bitcast.31), calls=%async_computation.1 | async-start | bytes 8388608 | tf_op jit(solution)/shard_map/all_to_all | solution.py:144
  107.6 22.6 %shard_map.69 = f32[256,72]{1,0:T(8,128)} custom-call(f32[256,64]{1,0:T(8,128)} %get-tuple-element.61.c8_ref, f32[256,1]{1,0:T(8,128)} %copy.22.bias_ref, f32[16,64,1024]{2,1,0:T(8,128)} %all-to-all-done.2.xs_ref), custom_call_target="tpu_custom_call" | custom-call | tf_op jit(solution)/shard_map/pallas_call | solution.py:78
  130.2 35.2 %all-to-all-done.1.xs_ref = f32[16,64,1024]{2,1,0:T(8,128)} async-done(((f32[16,64,1024]{2,1,0:T(8,128)}), f32[16,64,1024]{2,1,0:T(8,128)}, u32[]{:S(2)}, u32[]{:S(2)}) %all-to-all-start.1) | async-done | bytes 4194336 | tf_op jit(solution)/shard_map/all_to_all | solution.py:144
  165.4 27.7 %shard_map.68 = f32[256,72]{1,0:T(8,128)} custom-call(f32[256,64]{1,0:T(8,128)} %get-tuple-element.61.c8_ref, f32[256,1]{1,0:T(8,128)} %copy.22.bias_ref, f32[16,64,1024]{2,1,0:T(8,128)} %all-to-all-done.1.xs_ref), custom_call_target="tpu_custom_call" | custom-call | tf_op jit(solution)/shard_map/pallas_call | solution.py:78
  193.1 0.9 add.78
  194.1 0.8 broadcast_in_dim.15
  194.9 7.1 %all-to-all-start.3 = ((f32[8,256,72]{1,2,0:T(8,128)}), f32[8,256,72]{1,2,0:T(8,128)S(1)}, u32[]{:S(2)}, u32[]{:S(2)}) async-start(f32[8,256,72]{1,2,0:T(8,128)} %broadcast_in_dim.15), calls=%async_computation.3 | async-start | bytes 1179648 | tf_op jit(solution)/shard_map/all_to_all | solution.py:120
  202.0 4.7 %constant_dynamic-update-slice_fusion.1 = f32[32,64,1024]{2,1,0:T(8,128)} fusion(f32[16,64,1024]{2,1,0:T(8,128)} %all-to-all-done.1.xs_ref), kind=kLoop, calls=%fused_computation.40 | loop fusion | bytes 8388608
  206.7 4.7 %constant_dynamic-update-slice_fusion.xs_ref = f32[32,64,1024]{2,1,0:T(8,128)} fusion(f32[32,64,1024]{2,1,0:T(8,128)} %constant_dynamic-update-slice_fusion.1, f32[16,64,1024]{2,1,0:T(8,128)} %all-to-all-done.2.xs_ref), kind=kLoop, calls=%fused_computation.39 | loop fusion | bytes 8388608 | tf_op jit(solution)/shard_map/concatenate | solution.py:153
  213.4 122.8 %while.10 = (s32[]{:T(128)}, f32[256,64]{1,0:T(8,128)S(1)}, f32[32,64,1024]{2,1,0:T(8,128)}, f32[256]{0:T(256)S(1)}, s32[]{:T(128)}) while((s32[]{:T(128)}, f32[256,64]{1,0:T(8,128)S(1)}, f32[32,64,1024]{2,1,0:T(8,128)}, f32[256]{0:T(256)S(1)}, s32[]{:T(128)}) %tuple.41), condition=%wide.region_3.5_spmd, body=%wide.region_1.0_spmd.sunk | while | flops 211202 | bytes 3907677 | solution.py:161
  214.1 0.8 copy.49.bias_ref
  214.9 43.3 %eval_jaxpr.1 = f32[256,72]{1,0:T(8,128)} custom-call(f32[256,64]{1,0:T(8,128)} %broadcast_multiply_fusion.7.c8_ref, f32[256,1]{1,0:T(8,128)} %copy.49.bias_ref, f32[32,64,1024]{2,1,0:T(8,128)} %get-tuple-element.103.xs_ref), custom_call_target="tpu_custom_call" | custom-call | tf_op jit(solution)/shard_map/while/body/eval_jaxpr/pallas_call | solution.py:78
  258.1 1.0 copy.50
  259.1 0.9 broadcast_in_dim.54
  260.0 4.4 %all-to-all-start = ((f32[8,256,72]{1,2,0:T(8,128)}), f32[8,256,72]{1,2,0:T(8,128)S(1)}, u32[]{:S(2)}, u32[]{:S(2)}) async-start(f32[8,256,72]{1,2,0:T(8,128)} %broadcast_in_dim.54), calls=%async_computation | async-start | bytes 1179648 | tf_op jit(solution)/shard_map/while/body/eval_jaxpr/all_to_all | solution.py:120
  264.5 10.0 %all-to-all-done = f32[8,256,72]{1,2,0:T(8,128)S(1)} async-done(((f32[8,256,72]{1,2,0:T(8,128)}), f32[8,256,72]{1,2,0:T(8,128)S(1)}, u32[]{:S(2)}, u32[]{:S(2)}) %all-to-all-start) | async-done | bytes 589856 | tf_op jit(solution)/shard_map/while/body/eval_jaxpr/all_to_all | solution.py:120
  275.5 0.8 copy.49.bias_ref
  276.3 43.3 %eval_jaxpr.1 = f32[256,72]{1,0:T(8,128)} custom-call(f32[256,64]{1,0:T(8,128)} %broadcast_multiply_fusion.7.c8_ref, f32[256,1]{1,0:T(8,128)} %copy.49.bias_ref, f32[32,64,1024]{2,1,0:T(8,128)} %get-tuple-element.103.xs_ref), custom_call_target="tpu_custom_call" | custom-call | tf_op jit(solution)/shard_map/while/body/eval_jaxpr/pallas_call | solution.py:78
  319.6 1.0 copy.50
  320.5 0.9 broadcast_in_dim.54
  321.5 4.4 %all-to-all-start = ((f32[8,256,72]{1,2,0:T(8,128)}), f32[8,256,72]{1,2,0:T(8,128)S(1)}, u32[]{:S(2)}, u32[]{:S(2)}) async-start(f32[8,256,72]{1,2,0:T(8,128)} %broadcast_in_dim.54), calls=%async_computation | async-start | bytes 1179648 | tf_op jit(solution)/shard_map/while/body/eval_jaxpr/all_to_all | solution.py:120
  325.9 10.0 %all-to-all-done = f32[8,256,72]{1,2,0:T(8,128)S(1)} async-done(((f32[8,256,72]{1,2,0:T(8,128)}), f32[8,256,72]{1,2,0:T(8,128)S(1)}, u32[]{:S(2)}, u32[]{:S(2)}) %all-to-all-start) | async-done | bytes 589856 | tf_op jit(solution)/shard_map/while/body/eval_jaxpr/all_to_all | solution.py:120
  337.6 0.8 copy.34.bias_ref
  338.4 33.4 %shard_map.70 = f32[1,32768]{1,0:T(1,128)} custom-call(f32[256,64]{1,0:T(8,128)} %get-tuple-element.59.c8_ref, f32[256,1]{1,0:T(8,128)} %copy.34.bias_ref, f32[32,64,1024]{2,1,0:T(8,128)} %constant_dynamic-update-slice_fusion.xs_ref), custom_call_target="tpu_custom_call" | custom-call | tf_op jit(solution)/shard_map/pallas_call | solution.py:78
  372.3 1.9 reduce.5
  374.3 0.9 reshape.64
  (46 shorter events, 8.9 us)
Async XLA Ops:
  30.0 71.1 %all-to-all-start.2 = ((f32[16,64,1024]{2,1,0:T(8,128)}), f32[16,64,1024]{2,1,0:T(8,128)}, u32[]{:S(2)}, u32[]{:S(2)}) async-start(f32[16,64,1024]{2,1,0:T(8,128)} %bitcast.32), calls=%async_computation.2 | async-start | bytes 8388608 | tf_op jit(solution)/shard_map/all_to_all | solution.py:144
  101.1 4.9 %copy-start.1 = (f32[1,256,64]{1,2,0:T(8,128)S(1)}, f32[1,256,64]{1,2,0:T(8,128)}, u32[]{:S(2)}) copy-start(f32[1,256,64]{1,2,0:T(8,128)} %param.13) | copy-start | bytes 196612
  101.1 64.3 %all-to-all-start.1 = ((f32[16,64,1024]{2,1,0:T(8,128)}), f32[16,64,1024]{2,1,0:T(8,128)}, u32[]{:S(2)}, u32[]{:S(2)}) async-start(f32[16,64,1024]{2,1,0:T(8,128)} %bitcast.31), calls=%async_computation.1 | async-start | bytes 8388608 | tf_op jit(solution)/shard_map/all_to_all | solution.py:144
  130.2 62.9 %copy-start = (f32[256,72]{1,0:T(8,128)S(1)}, f32[256,72]{1,0:T(8,128)}, u32[]{:S(2)}) copy-start(f32[256,72]{1,0:T(8,128)} %shard_map.69) | copy-start | bytes 221188
  194.9 17.2 %all-to-all-start.3 = ((f32[8,256,72]{1,2,0:T(8,128)}), f32[8,256,72]{1,2,0:T(8,128)S(1)}, u32[]{:S(2)}, u32[]{:S(2)}) async-start(f32[8,256,72]{1,2,0:T(8,128)} %broadcast_in_dim.15), calls=%async_computation.3 | async-start | bytes 1179648 | tf_op jit(solution)/shard_map/all_to_all | solution.py:120
  260.0 14.5 %all-to-all-start = ((f32[8,256,72]{1,2,0:T(8,128)}), f32[8,256,72]{1,2,0:T(8,128)S(1)}, u32[]{:S(2)}, u32[]{:S(2)}) async-start(f32[8,256,72]{1,2,0:T(8,128)} %broadcast_in_dim.54), calls=%async_computation | async-start | bytes 1179648 | tf_op jit(solution)/shard_map/while/body/eval_jaxpr/all_to_all | solution.py:120
  321.5 14.5 %all-to-all-start = ((f32[8,256,72]{1,2,0:T(8,128)}), f32[8,256,72]{1,2,0:T(8,128)S(1)}, u32[]{:S(2)}, u32[]{:S(2)}) async-start(f32[8,256,72]{1,2,0:T(8,128)} %broadcast_in_dim.54), calls=%async_computation | async-start | bytes 1179648 | tf_op jit(solution)/shard_map/while/body/eval_jaxpr/all_to_all | solution.py:120
